TPU v7x, 32 devices: a whole 2x2x4 slice. The times are simulated.
32 devices in a mesh: dp: 4 (over z), vocab: 8 (over y, x, core).
Axes of the slice: x: 2, y: 2, z: 4, core: 2. Of those that a mesh axis runs over, the one named last changes fastest.
Arguments:
- hidden: bfloat16 [512, 8192], P('dp', 'vocab'), may hold values from -8 to 8
- out_weight: bfloat16 [19456, 8192], P('vocab', 'dp'), may hold values from -0.397747564 to 0.397747564
- token_blocks: int32 [8, 4, 16], P('vocab'), may hold values from 0 to 18, as said below
- counts: int32 [8, 4], P('vocab'), may hold values from 4 to 16, as said below
Outputs:
- allowed_logprob: float32 [8, 4, 16, 128, 128], P('vocab', 'dp')
- expected: float32 [512, 8192], P('vocab', 'dp')
Inputs may be any that keep to these rules, and one draw needn't show every extreme that they name: token_blocks[j, b, s] names one of the 19 token blocks of shard j; the entries of one list are distinct; slots at or past counts[j, b] carry no meaning. `counts`: for every beam block, some shard allows exactly 16 slots.
All inputs are finite; a program needn't handle non-finite values.
Results may differ from a plain program's by a relative error of at most 0.0021.
Values may be sent and summed in bfloat16 or wider, within the bound.
No kernel may reach another device: no remote copies, remote signals or barrier semaphores. Data moves between devices by JAX's collectives and lax.ppermute only.
A program may use at most 128 MiB of HBM per device.

v0:
```python
import jax
import jax.numpy as jnp
from jax import lax
from jax.sharding import PartitionSpec as P

TB = 128
BB = 128
MOST = 16


def per_device(hidden, out_weight, token_blocks, counts):
    vocab_here, columns_here = out_weight.shape
    width = hidden.shape[1] * lax.psum(1, "vocab")
    n_tb = vocab_here // TB
    block_lists = token_blocks[0]
    block_counts = counts[0]
    n_blk = block_lists.shape[0]
    own_blocks = hidden.shape[0] // BB
    first_block = lax.axis_index("dp") * own_blocks
    own_counts = lax.dynamic_slice_in_dim(block_counts, first_block, own_blocks, 0)
    beam_rows = lax.all_gather(hidden, "vocab", axis=1, tiled=True)
    beam_columns = lax.all_to_all(beam_rows, "dp", split_axis=1, concat_axis=0, tiled=True)
    with jax.named_scope("dense_logits"):
        full = jnp.einsum("bd,vd->bv", beam_columns, out_weight, preferred_element_type=jnp.float32)
        full4 = full.reshape(n_blk, BB, n_tb, TB)
        rows = jnp.arange(n_blk, dtype=jnp.int32)[:, None]
        picked = full4[rows, :, block_lists, :]
    logits = lax.psum_scatter(picked, "dp", scatter_dimension=0, tiled=True)
    with jax.named_scope("softmax_stats"):
        live = jnp.arange(MOST, dtype=jnp.int32)[None, :] < own_counts[:, None]
        live_mask = live[:, :, None, None]
        masked = jnp.where(live_mask, logits, -jnp.inf)
        local_max = jnp.max(masked, axis=(1, 3))
        local_total = jnp.sum(jnp.exp(masked - local_max[:, None, :, None]), axis=(1, 3))
        stats = lax.all_gather(jnp.stack([local_max, local_total]), "vocab", axis=0)
        beam_max = jnp.max(stats[:, 0], axis=0)
        beam_total = jnp.sum(stats[:, 1] * jnp.exp(stats[:, 0] - beam_max[None]), axis=0)
        shifted = logits - beam_max[:, None, :, None] - jnp.log(beam_total)[:, None, :, None]
        allowed_logprob = jnp.where(live_mask, shifted, 0.0)
        probabilities = jnp.where(live_mask, jnp.exp(shifted), 0.0).astype(jnp.bfloat16)
    prob_part = lax.all_gather(probabilities, "dp", axis=0, tiled=True)
    with jax.named_scope("dense_expected"):
        onehot = (
            block_lists[:, :, None] == jnp.arange(n_tb, dtype=jnp.int32)[None, None, :]
        ).astype(jnp.bfloat16)
        spread = jnp.einsum(
            "bsk,bsrt->brkt", onehot, prob_part, preferred_element_type=jnp.float32
        ).astype(jnp.bfloat16)
        embedding_part = jnp.einsum(
            "bv,vd->bd",
            spread.reshape(n_blk * BB, n_tb * TB),
            out_weight,
            preferred_element_type=jnp.float32,
        )
    summed = lax.psum_scatter(embedding_part, "vocab", scatter_dimension=0, tiled=True)
    squares = lax.psum(jnp.sum(summed * summed, axis=1), "dp")
    expected = summed * lax.rsqrt(squares / width + 1e-06)[:, None]
    return (allowed_logprob[None], expected)


def solution(mesh):
    in_specs = (P("dp", "vocab"), P("vocab", "dp"), P("vocab", None, None), P("vocab", None))
    out_specs = (P("vocab", "dp", None, None, None), P("vocab", "dp"))
    return jax.shard_map(
        per_device, mesh=mesh, in_specs=in_specs, out_specs=out_specs, check_vma=False
    )
```

profile of v0, /device:TPU:0, one launch (start us, length us, event | category | flops | bytes accessed | tf_op | source)
XLA Modules:
  0.0 333.0 jit_solution(18080191292290261255)
XLA Ops:
  7.2 0.0 copy-start
  7.2 0.0 all-gather.4.cloned.1.call-start
  7.2 1.8 copy.15
  9.0 0.0 all-gather.4.cloned.1.call-update
  9.0 31.9 %all-gather.4.cloned.1.call-done = bf16[128,8192]{0,1:T(8,128)(2,1)} async-done(((bf16[128,1024]{0,1:T(8,128)(2,1)}), bf16[128,8192]{0,1:T(8,128)(2,1)}) %all-gather.4.cloned.1.call-update) | async-done | bytes 2097168 | tf_op jit(solution)/shard_map/all_gather | solution.py:21
  41.0 0.0 copy-start.1
  41.0 4.0 %copy.16 = bf16[128,4,2048]{2,0,1:T(8,128)(2,1)} copy(bf16[128,4,2048]{0,2,1:T(8,128)(2,1)} %bitcast.42) | data formatting | bytes 4194304 | tf_op jit(solution)/shard_map/all_to_all | solution.py:22
  45.0 4.6 %all-to-all-start = ((bf16[128,4,2048]{2,0,1:T(8,128)(2,1)}), bf16[128,4,2048]{2,0,1:T(8,128)(2,1)S(1)}, u32[]{:S(2)}, u32[]{:S(2)}) async-start(bf16[128,4,2048]{2,0,1:T(8,128)(2,1)} %copy.16), calls=%async_computation | async-start | bytes 4194304 | tf_op jit(solution)/shard_map/all_to_all | solution.py:22
  49.6 0.0 reduce-scatter.3.cloned.1.call-start
  49.6 0.0 copy-done.1
  49.6 0.1 reshape.130
  49.7 48.5 %all-to-all-done = bf16[128,4,2048]{2,0,1:T(8,128)(2,1)S(1)} async-done(((bf16[128,4,2048]{2,0,1:T(8,128)(2,1)}), bf16[128,4,2048]{2,0,1:T(8,128)(2,1)S(1)}, u32[]{:S(2)}, u32[]{:S(2)}) %all-to-all-start) | async-done | bytes 2097184 | tf_op jit(solution)/shard_map/all_to_all | solution.py:22
  98.2 9.9 %fusion.3 = f32[4,128,19,128]{3,1,2,0:T(8,128)} fusion(bf16[19,128,2048,1]{2,1,0,3:T(8,128)(2,1)} %bitcast.50, bf16[128,4,2048]{2,0,1:T(8,128)(2,1)S(1)} %all-to-all-done), kind=kOutput, calls=%fused_computation.5 | convolution fusion | flops 5100273664 | bytes 17039360 | tf_op jit(solution)/shard_map/dense_logits/bd,vd->bv/dot_general | solution.py:24
  108.1 5.3 %gather_fusion = f32[64,128,128]{2,1,0:T(8,128)} fusion(f32[4,128,19,128]{3,1,2,0:T(8,128)} %fusion.3, s32[64]{0:T(128)S(1)} %reshape.130), kind=kCustom, calls=%fused_computation | custom fusion | bytes 8389120 | tf_op jit(solution)/shard_map/dense_logits/gather | solution.py:27
  113.4 0.0 reduce-scatter.3.cloned.1.call-update
  113.4 0.0 all-gather.6.cloned.1.call-start
  113.4 0.0 copy-done
  113.4 0.6 constant_dynamic-slice_fusion
  114.0 0.6 iota_compare_fusion.1
  114.7 73.8 %reduce-scatter.3.cloned.1.call-done = f32[1,16,128,128]{3,2,1,0:T(8,128)} async-done(((f32[4,16,128,128]{3,2,1,0:T(8,128)}), f32[1,16,128,128]{3,2,1,0:T(8,128)}) %reduce-scatter.3.cloned.1.call-update) | async-done | bytes 1048592 | tf_op jit(solution)/shard_map/reduce_scatter | solution.py:28
  188.5 1.4 select_reduce_fusion
  189.9 1.6 exponential_reduce_fusion
  191.5 8.9 %all-gather = f32[16,1,128]{2,1,0:T(1,128)S(1)} all-gather(f32[2,1,128]{2,1,0:T(1,128)S(1)} %pad_maximum_fusion), channel_id=2, replica_groups=mesh['dp'=4,'vocab'=8] {'vocab'}, dimensions={0}, use_global_device_ids=true | all-gather | bytes 9216 | tf_op jit(solution)/shard_map/softmax_stats/all_gather | solution.py:35
  200.4 2.8 select_convert_fusion
  203.2 0.0 all-gather.6.cloned.1.call-update
  203.3 0.0 reduce-scatter.5.cloned.1.call-start
  203.3 45.4 %all-gather.6.cloned.1.call-done = bf16[4,16,128,128]{3,2,1,0:T(8,128)(2,1)} async-done(((bf16[1,16,128,128]{3,2,1,0:T(8,128)(2,1)}), bf16[4,16,128,128]{3,2,1,0:T(8,128)(2,1)}) %all-gather.6.cloned.1.call-update) | async-done | bytes 2097168 | tf_op jit(solution)/shard_map/all_gather | solution.py:41
  248.7 3.3 convolution_convert_fusion
  251.9 9.5 %fusion = f32[512,2048]{1,0:T(8,128)} fusion(bf16[2432,2048]{1,0:T(8,128)(2,1)} %param.5, bf16[64,8,19,128]{3,2,1,0:T(8,128)(2,1)S(1)} %bitcast.41), kind=kOutput, calls=%fused_computation.1 | convolution fusion | flops 5100273664 | bytes 16646144 | tf_op jit(solution)/shard_map/dense_expected/bv,vd->bd/dot_general | solution.py:49
  261.5 0.0 reduce-scatter.5.cloned.1.call-update
  261.5 50.1 %reduce-scatter.5.cloned.1.call-done = f32[64,2048]{1,0:T(8,128)} async-done(((f32[512,2048]{1,0:T(8,128)}), f32[64,2048]{1,0:T(8,128)}) %reduce-scatter.5.cloned.1.call-update) | async-done | bytes 524304 | tf_op jit(solution)/shard_map/reduce_scatter | solution.py:55
  311.6 1.2 multiply_reduce_fusion
  312.8 11.7 %psum.7 = f32[64]{0:T(128)S(1)} all-reduce(f32[64]{0:T(128)S(1)} %multiply_reduce_fusion), channel_id=1, replica_groups=mesh['dp'=4,'vocab'=8] {'dp'}, use_global_device_ids=true, to_apply=%region_7.8 | all-reduce | flops 64 | bytes 512 | tf_op jit(solution)/shard_map/psum | solution.py:56
  324.5 1.9 broadcast_multiply_fusion
  (7 shorter events, 0.1 us)
Async XLA Ops:
  7.2 106.3 %copy-start = (s32[1,4]{1,0:T(1,128)S(1)}, s32[1,4]{1,0:T(1,128)}, u32[]{:S(2)}) copy-start(s32[1,4]{1,0:T(1,128)} %param.7) | copy-start | bytes 52
  7.2 33.8 %all-gather.4.cloned.1.call-start = ((), (), s32[]{:S(2)}) async-start(), calls=%async_computation.3 | async-start | bytes 2359296 | tf_op jit(solution)/shard_map/all_gather | solution.py:21
  41.0 8.6 %copy-start.1 = (s32[1,4,16]{2,1,0:T(4,128)S(1)}, s32[1,4,16]{2,1,0:T(4,128)}, u32[]{:S(2)}) copy-start(s32[1,4,16]{2,1,0:T(4,128)} %param.6) | copy-start | bytes 772
  45.0 53.2 %all-to-all-start = ((bf16[128,4,2048]{2,0,1:T(8,128)(2,1)}), bf16[128,4,2048]{2,0,1:T(8,128)(2,1)S(1)}, u32[]{:S(2)}, u32[]{:S(2)}) async-start(bf16[128,4,2048]{2,0,1:T(8,128)(2,1)} %copy.16), calls=%async_computation | async-start | bytes 4194304 | tf_op jit(solution)/shard_map/all_to_all | solution.py:22
  49.6 138.9 %reduce-scatter.3.cloned.1.call-start = ((), (), s32[]{:S(2)}) async-start(), calls=%async_computation.4 | async-start | bytes 5242880 | tf_op jit(solution)/shard_map/reduce_scatter | solution.py:28
  113.4 135.3 %all-gather.6.cloned.1.call-start = ((), (), s32[]{:S(2)}) async-start(), calls=%async_computation.5 | async-start | bytes 2621440 | tf_op jit(solution)/shard_map/all_gather | solution.py:41
  203.3 108.3 %reduce-scatter.5.cloned.1.call-start = ((), (), s32[]{:S(2)}) async-start(), calls=%async_computation.6 | async-start | bytes 4718592 | tf_op jit(solution)/shard_map/reduce_scatter | solution.py:55
Sparse Core Ops, SparseCore 0:
  10.4 30.4 all-gather.3
  113.5 74.9 reduce-scatter.2
  203.4 45.2 all-gather.5
  261.6 49.9 reduce-scatter.4
where the time goes:
time: 334 us; the launch traced here: 333 us
  waiting for transfers between devices  250 us (75%)
  matrix products  22.7 us (7%)
  blocking collectives  20.6 us (6%)
  between operations  13.8 us (4%)
  local copies, waits for them, and re-layouts  11.8 us (4%)
  other arithmetic  9.65 us (3%)
  starting transfers between devices  4.72 us (1%)
    reduce_scatter x1, waiting for transfers between devices, per_device(): logits = lax.psum_scatter(picked, 'dp', scatter_dimension=0, tiled=True)  73.8 us
    reduce_scatter x1, waiting for transfers between devices, per_device(): lax.psum_scatter(embedding_part, 'vocab', scatter_dimension=0, tiled=True)  50.1 us
    all_to_all x1, waiting for transfers between devices, per_device(): lax.all_to_all(beam_rows, 'dp', split_axis=1, concat_axis=0, tiled=True)  48.5 us
    all_gather x1, waiting for transfers between devices, per_device(): prob_part = lax.all_gather(probabilities, 'dp', axis=0, tiled=True)  45.4 us
    all_gather x1, waiting for transfers between devices, per_device(): beam_rows = lax.all_gather(hidden, 'vocab', axis=1, tiled=True)  31.9 us
    psum x1, blocking collectives, per_device(): squares = lax.psum(jnp.sum(summed * summed, axis=1), 'dp')  11.7 us
    dot_general x1, matrix products, per_device(): jnp.einsum('bd,vd->bv', beam_columns, out_weight, preferred_element_type=...  9.91 us
    dot_general x1, matrix products, per_device(): jnp.einsum('bv,vd->bd', spread.reshape(n_blk * BB, n_tb * TB), out_weight...  9.53 us
  transfers between devices with their start and end apart: 5, of which 5 were waited for; matrix products, arithmetic and copies ran while one was open for 0% of the time, Pallas kernels for 0%

commit v1 on v0

--- a/solution.py
+++ b/solution.py
@@ -38,7 +38,22 @@
         shifted = logits - beam_max[:, None, :, None] - jnp.log(beam_total)[:, None, :, None]
         allowed_logprob = jnp.where(live_mask, shifted, 0.0)
         probabilities = jnp.where(live_mask, jnp.exp(shifted), 0.0).astype(jnp.bfloat16)
-    prob_part = lax.all_gather(probabilities, "dp", axis=0, tiled=True)
+    ways, here, step = (lax.axis_size("dp"), lax.axis_index("dp"), probabilities.shape[0])
+    shape = [n * ways if d == 0 else n for d, n in enumerate(probabilities.shape)]
+    prob_part = lax.dynamic_update_slice_in_dim(
+        jnp.zeros(shape, probabilities.dtype), probabilities, here * step, axis=0
+    )
+    going_up = going_down = probabilities
+    for far in range(1, ways // 2 + 1):
+        going_up = lax.ppermute(going_up, "dp", [(d, (d + 1) % ways) for d in range(ways)])
+        prob_part = lax.dynamic_update_slice_in_dim(
+            prob_part, going_up, (here - far) % ways * step, axis=0
+        )
+        if 2 * far < ways:
+            going_down = lax.ppermute(going_down, "dp", [(d, (d - 1) % ways) for d in range(ways)])
+            prob_part = lax.dynamic_update_slice_in_dim(
+                prob_part, going_down, (here + far) % ways * step, axis=0
+            )
     with jax.named_scope("dense_expected"):
         onehot = (
             block_lists[:, :, None] == jnp.arange(n_tb, dtype=jnp.int32)[None, None, :]

time: 334 us -> 323 us (0.967)
  waiting for transfers between devices: 250 us -> 227 us
  starting transfers between devices: 4.72 us -> 18.6 us
    all_gather x1 -> x0, waiting for transfers between devices: 45.4 us -> none  [per_device(): prob_part = lax.all_gather(probabilities, 'dp', axis=0, tiled=True)]
    ppermute x0 -> x3, waiting for transfers between devices: none -> 23.2 us  [the longest x2 23.2 us: per_device(): lax.ppermute(going_up, 'dp', [(d, (d + 1) % ways) for d in range(ways)])]
    ppermute x0 -> x3, starting transfers between devices: none -> 13.8 us  [the longest x2 11.5 us: per_device(): lax.ppermute(going_up, 'dp', [(d, (d + 1) % ways) for d in range(ways)])]
  transfers between devices with their start and end apart: 5 -> 7, of which waited for: 5 -> 6; matrix products, arithmetic and copies ran while one was open for 0% -> 1% of each run, Pallas kernels for 0% -> 0%
where the time goes in v1:
time: 323 us; the launch traced here: 322 us
  waiting for transfers between devices  227 us (70%)
  blocking collectives  20.6 us (6%)
  matrix products  20.5 us (6%)
  starting transfers between devices  18.6 us (6%)
  between operations  13.8 us (4%)
  local copies, waits for them, and re-layouts  13.5 us (4%)
  other arithmetic  8.34 us (3%)
    reduce_scatter x1, waiting for transfers between devices, per_device(): logits = lax.psum_scatter(picked, 'dp', scatter_dimension=0, tiled=True)  73.8 us
    reduce_scatter x1, waiting for transfers between devices, per_device(): lax.psum_scatter(embedding_part, 'vocab', scatter_dimension=0, tiled=True)  49.5 us
    all_to_all x1, waiting for transfers between devices, per_device(): lax.all_to_all(beam_rows, 'dp', split_axis=1, concat_axis=0, tiled=True)  48.5 us
    all_gather x1, waiting for transfers between devices, per_device(): beam_rows = lax.all_gather(hidden, 'vocab', axis=1, tiled=True)  31.9 us
    ppermute x2, waiting for transfers between devices, per_device(): lax.ppermute(going_up, 'dp', [(d, (d + 1) % ways) for d in range(ways)])  23.2 us
    psum x1, blocking collectives, per_device(): squares = lax.psum(jnp.sum(summed * summed, axis=1), 'dp')  11.7 us
    ppermute x2, starting transfers between devices, per_device(): lax.ppermute(going_up, 'dp', [(d, (d + 1) % ways) for d in range(ways)])  11.5 us
    dot_general x1, matrix products, per_device(): jnp.einsum('bd,vd->bv', beam_columns, out_weight, preferred_element_type=...  9.91 us
  transfers between devices with their start and end apart: 7, of which 6 were waited for; matrix products, arithmetic and copies ran while one was open for 1% of the time, Pallas kernels for 0%

profile of v1, /device:TPU:0, one launch (start us, length us, event | category | flops | bytes accessed | tf_op | source)
XLA Modules:
  0.0 322.5 jit_solution(12057733141031823585)
XLA Ops:
  7.2 0.0 copy-start
  7.2 0.0 all-gather.3.cloned.1.call-start
  7.2 1.8 copy.19
  9.0 0.0 all-gather.3.cloned.1.call-update
  9.0 31.9 %all-gather.3.cloned.1.call-done = bf16[128,8192]{0,1:T(8,128)(2,1)} async-done(((bf16[128,1024]{0,1:T(8,128)(2,1)}), bf16[128,8192]{0,1:T(8,128)(2,1)}) %all-gather.3.cloned.1.call-update) | async-done | bytes 2097168 | tf_op jit(solution)/shard_map/all_gather | solution.py:21
  41.0 4.0 %copy.20 = bf16[128,4,2048]{2,0,1:T(8,128)(2,1)} copy(bf16[128,4,2048]{0,2,1:T(8,128)(2,1)} %bitcast.43) | data formatting | bytes 4194304 | tf_op jit(solution)/shard_map/all_to_all | solution.py:22
  45.0 0.0 copy-start.2
  45.0 4.7 %all-to-all-start = ((bf16[128,4,2048]{2,0,1:T(8,128)(2,1)}), bf16[128,4,2048]{2,0,1:T(8,128)(2,1)S(1)}, u32[]{:S(2)}, u32[]{:S(2)}) async-start(bf16[128,4,2048]{2,0,1:T(8,128)(2,1)} %copy.20), calls=%async_computation | async-start | bytes 4194304 | tf_op jit(solution)/shard_map/all_to_all | solution.py:22
  49.7 0.0 reduce-scatter.3.cloned.1.call-start
  49.7 0.0 copy-done.2
  49.7 0.1 reshape.130
  49.8 48.5 %all-to-all-done = bf16[128,4,2048]{2,0,1:T(8,128)(2,1)S(1)} async-done(((bf16[128,4,2048]{2,0,1:T(8,128)(2,1)}), bf16[128,4,2048]{2,0,1:T(8,128)(2,1)S(1)}, u32[]{:S(2)}, u32[]{:S(2)}) %all-to-all-start) | async-done | bytes 2097184 | tf_op jit(solution)/shard_map/all_to_all | solution.py:22
  98.3 9.9 %fusion.3 = f32[4,128,19,128]{3,1,2,0:T(8,128)} fusion(bf16[19,128,2048,1]{2,1,0,3:T(8,128)(2,1)} %bitcast.51, bf16[128,4,2048]{2,0,1:T(8,128)(2,1)S(1)} %all-to-all-done), kind=kOutput, calls=%fused_computation.5 | convolution fusion | flops 5100273664 | bytes 17039360 | tf_op jit(solution)/shard_map/dense_logits/bd,vd->bv/dot_general | solution.py:24
  108.2 5.3 %gather_fusion = f32[64,128,128]{2,1,0:T(8,128)} fusion(f32[4,128,19,128]{3,1,2,0:T(8,128)} %fusion.3, s32[64]{0:T(128)S(1)} %reshape.130), kind=kCustom, calls=%fused_computation | custom fusion | bytes 8389120 | tf_op jit(solution)/shard_map/dense_logits/gather | solution.py:27
  113.5 0.0 reduce-scatter.3.cloned.1.call-update
  113.5 0.0 reduce-scatter.5.cloned.1.call-start
  113.6 0.0 copy-done
  113.6 0.6 constant_dynamic-slice_fusion
  114.2 0.6 iota_compare_fusion.1
  114.8 73.8 %reduce-scatter.3.cloned.1.call-done = f32[1,16,128,128]{3,2,1,0:T(8,128)} async-done(((f32[4,16,128,128]{3,2,1,0:T(8,128)}), f32[1,16,128,128]{3,2,1,0:T(8,128)}) %reduce-scatter.3.cloned.1.call-update) | async-done | bytes 1048592 | tf_op jit(solution)/shard_map/reduce_scatter | solution.py:28
  188.6 0.0 copy-start.1
  188.6 1.5 select_reduce_fusion
  190.1 1.6 exponential_reduce_fusion
  191.7 8.9 %all-gather = f32[16,1,128]{2,1,0:T(1,128)S(1)} all-gather(f32[2,1,128]{2,1,0:T(1,128)S(1)} %pad_maximum_fusion), channel_id=2, replica_groups=mesh['dp'=4,'vocab'=8] {'vocab'}, dimensions={0}, use_global_device_ids=true | all-gather | bytes 9216 | tf_op jit(solution)/shard_map/softmax_stats/all_gather | solution.py:35
  200.6 0.0 copy-done.1
  200.7 1.4 select_convert_fusion
  202.1 1.5 collective-permute-start
  203.5 2.3 collective-permute-start.1
  205.9 12.8 %collective-permute-done = bf16[1,16,128,128]{3,2,1,0:T(8,128)(2,1)S(1)} collective-permute-done((bf16[1,16,128,128]{3,2,1,0:T(8,128)(2,1)S(1)}, bf16[1,16,128,128]{3,2,1,0:T(8,128)(2,1)S(1)}, u32[]{:S(2)}, u32[]{:S(2)}) %collective-permute-start) | collective-permute-done | bytes 524320 | tf_op jit(solution)/shard_map/ppermute | solution.py:48
  218.7 10.0 %collective-permute-start.2 = (bf16[1,16,128,128]{3,2,1,0:T(8,128)(2,1)S(1)}, bf16[1,16,128,128]{3,2,1,0:T(8,128)(2,1)S(1)}, u32[]{:S(2)}, u32[]{:S(2)}) collective-permute-start(bf16[1,16,128,128]{3,2,1,0:T(8,128)(2,1)S(1)} %collective-permute-done), channel_id=1, source_target_pairs={{0,8},{8,16},{16,24},{24,0},{1,9},{9,17},{17,25},{25,1},{2,10},{10... | collective-permute-start | bytes 1572872 | tf_op jit(solution)/shard_map/ppermute | solution.py:48
  228.7 0.3 broadcast_in_dim.49
  229.0 0.4 copy_dynamic-update-slice_fusion.3
  229.4 0.4 copy_dynamic-update-slice_fusion.2
  229.8 0.0 collective-permute-done.1
  229.8 0.4 copy_dynamic-update-slice_fusion.1
  230.2 10.4 %collective-permute-done.2 = bf16[1,16,128,128]{3,2,1,0:T(8,128)(2,1)S(1)} collective-permute-done((bf16[1,16,128,128]{3,2,1,0:T(8,128)(2,1)S(1)}, bf16[1,16,128,128]{3,2,1,0:T(8,128)(2,1)S(1)}, u32[]{:S(2)}, u32[]{:S(2)}) %collective-permute-start.2) | collective-permute-done | bytes 524320 | tf_op jit(solution)/shard_map/ppermute | solution.py:48
  240.6 0.4 copy_dynamic-update-slice_fusion
  240.9 1.1 convolution_convert_fusion
  242.0 9.5 %fusion = f32[512,2048]{1,0:T(8,128)} fusion(bf16[2432,2048]{1,0:T(8,128)(2,1)} %param.5, bf16[64,8,19,128]{3,2,1,0:T(8,128)(2,1)S(1)} %bitcast.42), kind=kOutput, calls=%fused_computation.1 | convolution fusion | flops 5100273664 | bytes 16646144 | tf_op jit(solution)/shard_map/dense_expected/bv,vd->bd/dot_general | solution.py:64
  251.5 0.0 reduce-scatter.5.cloned.1.call-update
  251.6 49.5 %reduce-scatter.5.cloned.1.call-done = f32[64,2048]{1,0:T(8,128)} async-done(((f32[512,2048]{1,0:T(8,128)}), f32[64,2048]{1,0:T(8,128)}) %reduce-scatter.5.cloned.1.call-update) | async-done | bytes 524304 | tf_op jit(solution)/shard_map/reduce_scatter | solution.py:70
  301.1 1.2 multiply_reduce_fusion
  302.3 11.7 %psum.7 = f32[64]{0:T(128)S(1)} all-reduce(f32[64]{0:T(128)S(1)} %multiply_reduce_fusion), channel_id=1, replica_groups=mesh['dp'=4,'vocab'=8] {'dp'}, use_global_device_ids=true, to_apply=%region_7.8 | all-reduce | flops 64 | bytes 512 | tf_op jit(solution)/shard_map/psum | solution.py:71
  314.0 1.9 broadcast_multiply_fusion
  (7 shorter events, 0.1 us)
Async XLA Ops:
  7.2 106.4 %copy-start = (s32[1,4]{1,0:T(1,128)S(1)}, s32[1,4]{1,0:T(1,128)}, u32[]{:S(2)}) copy-start(s32[1,4]{1,0:T(1,128)} %param.7) | copy-start | bytes 52
  7.2 33.8 %all-gather.3.cloned.1.call-start = ((), (), s32[]{:S(2)}) async-start(), calls=%async_computation.3 | async-start | bytes 2359296 | tf_op jit(solution)/shard_map/all_gather | solution.py:21
  45.0 4.7 %copy-start.2 = (s32[1,4,16]{2,1,0:T(4,128)S(1)}, s32[1,4,16]{2,1,0:T(4,128)}, u32[]{:S(2)}) copy-start(s32[1,4,16]{2,1,0:T(4,128)} %param.6) | copy-start | bytes 772
  45.0 53.3 %all-to-all-start = ((bf16[128,4,2048]{2,0,1:T(8,128)(2,1)}), bf16[128,4,2048]{2,0,1:T(8,128)(2,1)S(1)}, u32[]{:S(2)}, u32[]{:S(2)}) async-start(bf16[128,4,2048]{2,0,1:T(8,128)(2,1)} %copy.20), calls=%async_computation | async-start | bytes 4194304 | tf_op jit(solution)/shard_map/all_to_all | solution.py:22
  49.7 138.9 %reduce-scatter.3.cloned.1.call-start = ((), (), s32[]{:S(2)}) async-start(), calls=%async_computation.4 | async-start | bytes 5242880 | tf_op jit(solution)/shard_map/reduce_scatter | solution.py:28
  113.5 187.6 %reduce-scatter.5.cloned.1.call-start = ((), (), s32[]{:S(2)}) async-start(), calls=%async_computation.5 | async-start | bytes 4718592 | tf_op jit(solution)/shard_map/reduce_scatter | solution.py:70
  188.6 12.1 %copy-start.1 = (f32[1,16,128,128]{3,2,1,0:T(8,128)S(1)}, f32[1,16,128,128]{3,2,1,0:T(8,128)}, u32[]{:S(2)}) copy-start(f32[1,16,128,128]{3,2,1,0:T(8,128)} %reduce-scatter.3.cloned.1.call-done) | copy-start | bytes 3145732
  202.1 16.6 %collective-permute-start = (bf16[1,16,128,128]{3,2,1,0:T(8,128)(2,1)S(1)}, bf16[1,16,128,128]{3,2,1,0:T(8,128)(2,1)S(1)}, u32[]{:S(2)}, u32[]{:S(2)}) collective-permute-start(bf16[1,16,128,128]{3,2,1,0:T(8,128)(2,1)S(1)} %get-tuple-element.2), channel_id=1, source_target_pairs={{0,8},{8,16},{16,24},{24,0},{1,9},{9,17},{17,25},{25,1},{2,10},{10... | collective-permute-start | bytes 1572872 | tf_op jit(solution)/shard_map/ppermute | solution.py:48
  203.5 26.2 %collective-permute-start.1 = (bf16[1,16,128,128]{3,2,1,0:T(8,128)(2,1)S(1)}, bf16[1,16,128,128]{3,2,1,0:T(8,128)(2,1)S(1)}, u32[]{:S(2)}, u32[]{:S(2)}) collective-permute-start(bf16[1,16,128,128]{3,2,1,0:T(8,128)(2,1)S(1)} %get-tuple-element.2), channel_id=1, source_target_pairs={{0,24},{8,0},{16,8},{24,16},{1,25},{9,1},{17,9},{25,17},{2,26},{10... | collective-permute-start | bytes 1572872 | tf_op jit(solution)/shard_map/ppermute | solution.py:53
  218.7 21.8 %collective-permute-start.2 = (bf16[1,16,128,128]{3,2,1,0:T(8,128)(2,1)S(1)}, bf16[1,16,128,128]{3,2,1,0:T(8,128)(2,1)S(1)}, u32[]{:S(2)}, u32[]{:S(2)}) collective-permute-start(bf16[1,16,128,128]{3,2,1,0:T(8,128)(2,1)S(1)} %collective-permute-done), channel_id=1, source_target_pairs={{0,8},{8,16},{16,24},{24,0},{1,9},{9,17},{17,25},{25,1},{2,10},{10... | collective-permute-start | bytes 1572872 | tf_op jit(solution)/shard_map/ppermute | solution.py:48
Sparse Core Ops, SparseCore 0:
  10.4 30.4 all-gather.2
  113.6 74.9 reduce-scatter.2
  251.7 49.3 reduce-scatter.4
